TPU v7x, 32 devices: a whole 2x2x4 slice. The times are simulated.
32 devices in a mesh: win: 4 (over y, x), chan: 8 (over z, core).
Axes of the slice: x: 2, y: 2, z: 4, core: 2. Of those that a mesh axis runs over, the one named last changes fastest.
Arguments:
- source_traces: bfloat16 [4, 1024, 1536], P('win', 'chan'), may hold values from -60 to 60, as said below
- receiver_traces: bfloat16 [4, 8, 1536], P('win', 'chan'), may hold values from -60 to 60, as said below
- owners: int32 [4], replicated, may hold values from 0 to 7
- source_alive: int32 [1024], P('chan'), may hold values 0 or 1
- receiver_alive: int32 [8], P('chan'), may hold values 0 or 1
Outputs:
- gathers: float32 [4, 128, 8, 1501], P(None, 'win', 'chan')
Inputs may be any that keep to these rules, and one draw needn't show every extreme that they name: `source_traces`: trace samples. `receiver_traces`: trace samples.
All inputs are finite; a program needn't handle non-finite values. No bound on the sum of `source_alive` or of `receiver_alive` on one device may be relied on, other than what follows from the above.
Results may differ from a plain program's by a relative error of at most 0.0041.
Values may be sent and summed in bfloat16 or wider, within the bound.
No kernel may reach another device: no remote copies, remote signals or barrier semaphores. Data moves between devices by JAX's collectives and lax.ppermute only.
A program may use at most 64 MiB of HBM per device.

v0:
```python
import functools
import math

import jax
import jax.numpy as jnp
from jax import lax
from jax.experimental import pallas as pl
from jax.experimental.pallas import tpu as pltpu
from jax.sharding import Mesh, PartitionSpec as P

HALF = 750
STEPS = 4
CHUNK = 256

epsilon_energy = 1e-06


def spectral_flatten(traces):
    row_entries, length = traces.shape
    values = traces.astype(jnp.float32).reshape(row_entries, length // 64, 64)
    power = jnp.mean(values * values, axis=-1, keepdims=True)
    return (values * lax.rsqrt(power + epsilon_energy)).reshape(row_entries, length)


def corr_kernel(x_ref, p_ref, o_ref, *, nt, cols, lags, scale):
    n_win, m, _ = x_ref.shape
    width = CHUNK + cols
    acc = jnp.zeros((m, cols), jnp.float32)
    for w in range(n_win):
        for i in range(nt // CHUNK):
            t0 = i * CHUNK
            start = nt - CHUNK - t0
            v = p_ref[w, :, start:start + width]
            rows = jnp.broadcast_to(v, (CHUNK, width))
            rolled = pltpu.roll(rows, 0, 1, stride=1, stride_axis=0)
            band = rolled[:, CHUNK:CHUNK + cols].astype(jnp.bfloat16)
            acc = acc + jnp.dot(
                x_ref[w, :, t0:t0 + CHUNK], band, preferred_element_type=jnp.float32
            )
    o_ref[...] = (acc * scale)[:, :lags].reshape(m, 1, lags)


def correlate(x, p, lags, scale):
    n_win, m, nt = x.shape
    cols = p.shape[-1] - nt
    kern = functools.partial(corr_kernel, nt=nt, cols=cols, lags=lags, scale=scale)
    return pl.pallas_call(
        kern,
        out_shape=jax.ShapeDtypeStruct((m, 1, lags), jnp.float32),
        compiler_params=pltpu.CompilerParams(vmem_limit_bytes=48 * 1024 * 1024),
    )(x, p)


def body(source_traces, receiver_traces, owners, source_alive, receiver_alive):
    lag_count = 2 * HALF + 1
    n_win = lax.axis_size("win")
    n_core = lax.axis_size("core")
    nt = source_traces.shape[2]
    rows = source_traces.shape[1] // n_win
    half = rows // n_core
    cols = -(-lag_count // 128) * 128
    per = -(-nt // half)
    extra = -(-per // 128) * 128
    scale = 1.0 / math.sqrt(n_win * nt)

    own_white = (
        spectral_flatten(source_traces[0]) * source_alive.astype(jnp.float32)[:, None]
    ).astype(jnp.bfloat16)
    own_white = own_white[:, ::-1].reshape(n_win * n_core, half, nt)
    rcv_white = (
        spectral_flatten(receiver_traces[0]) * receiver_alive.astype(jnp.float32)[:, None]
    ).astype(jnp.bfloat16)
    rcv_rows = jnp.pad(rcv_white.reshape(-1), (0, half * per - nt)).reshape(half, per)
    rcv_rows = jnp.pad(rcv_rows, ((0, 0), (0, extra - per)))
    payload = jnp.concatenate(
        [own_white, jnp.broadcast_to(rcv_rows, (n_win * n_core, half, extra))], axis=2
    )
    got = lax.all_to_all(payload, ("win", "core"), 0, 0, tiled=True)
    got = got.reshape(n_win, n_core, half, nt + extra)

    my_core = lax.axis_index("core")
    my_chip = lax.axis_index("zz")
    n_chip = lax.axis_size("zz")
    src = got[..., :nt]
    chip_of = owners // n_core
    core_of = owners % n_core
    cores = jnp.arange(n_core, dtype=owners.dtype)
    chips = jnp.arange(n_chip, dtype=owners.dtype)
    wanted = jnp.any(
        (chip_of[:, None, None] == chips[None, :, None])
        & (core_of[:, None, None] == cores[None, None, :]),
        axis=0,
    )

    def ring_of(part):
        return jnp.stack([part] + [
            lax.ppermute(part, "zz", [(i, (i + j) % n_chip) for i in range(n_chip)])
            for j in range(1, n_chip)
        ])

    def steps_from(ring, pick_core):
        picked = []
        for k in range(STEPS):
            at = lax.rem(my_chip - chip_of[k] + n_chip, n_chip)
            block = lax.dynamic_index_in_dim(ring, at, 0, keepdims=False)
            if pick_core:
                block = lax.dynamic_index_in_dim(block, core_of[k], 1, keepdims=False)
            picked.append(block)
        return jnp.stack(picked, axis=1)

    def both_blocks(src):
        return steps_from(ring_of(src), True)

    def one_block(src):
        slot = jnp.argmax(wanted[my_chip]).astype(jnp.int32)
        part = lax.dynamic_index_in_dim(src, slot, 1, keepdims=False)
        return steps_from(ring_of(part), False)

    def one_double(c):
        def run(src):
            slot = jnp.argmax(wanted[my_chip]).astype(jnp.int32)
            part = lax.dynamic_index_in_dim(src, slot, 1, keepdims=False)
            first = steps_from(ring_of(part), False)
            extra = src[:, n_core - 1]
            second = jnp.where(my_chip == c, extra, jnp.zeros_like(extra))
            for j in range(1, n_chip):
                second = second + lax.ppermute(extra, "zz", [(c, (c + j) % n_chip)])
            late = owners == c * n_core + n_core - 1
            return jnp.where(late[None, :, None, None], second[:, None], first)
        return run

    doubles = jnp.sum(wanted.astype(jnp.int32), axis=1) == n_core
    n_doubles = jnp.sum(doubles.astype(jnp.int32))
    if n_chip <= 4 and n_core == 2:
        which = jnp.where(
            n_doubles == 0, 0,
            jnp.where(n_doubles == 1, 1 + jnp.argmax(doubles).astype(jnp.int32), n_chip + 1),
        )
        branches = [one_block] + [one_double(c) for c in range(n_chip)] + [both_blocks]
        mine_half = lax.switch(which, branches, src)
    else:
        mine_half = lax.cond(n_doubles == 0, one_block, both_blocks, src)
    other_half = lax.ppermute(mine_half, "core", [(0, 1), (1, 0)])
    blocks = jnp.where(
        my_core == 0,
        jnp.concatenate([mine_half, other_half], axis=2),
        jnp.concatenate([other_half, mine_half], axis=2),
    )
    x = blocks.reshape(n_win, STEPS * rows, nt)

    mine = lax.dynamic_index_in_dim(got, my_core, axis=1, keepdims=False)
    rcv_all = mine[:, :, nt:nt + per].reshape(n_win, half * per)[:, :nt]
    padded = jnp.pad(
        rcv_all.astype(jnp.float32), ((0, 0), (HALF + 1, cols - HALF - 1))
    )[:, None, :]

    out = correlate(x, padded, lag_count, scale)
    return out.reshape(STEPS, rows, 1, lag_count)


def solution(mesh):
    n_chan = mesh.shape["chan"]
    devices = mesh.devices.reshape(mesh.shape["win"], n_chan // 2, 2)
    sub = Mesh(devices, ("win", "zz", "core"))
    chan = ("zz", "core")
    placed = (P("win", chan, None), P("win", chan, None), P(), P(chan), P(chan))
    return jax.shard_map(
        body, mesh=sub, in_specs=placed, out_specs=P(None, "win", chan, None), check_vma=False
    )
```

profile of v0, /device:TPU:0, one launch (start us, length us, event | category | flops | bytes accessed | tf_op | source)
XLA Modules:
  0.0 49.8 jit_solution(8473842924998357394)
XLA Ops:
  0.7 0.7 %convert_element_type.77 = f32[128]{0:T(128)S(1)} convert(s32[128]{0:T(128)} %param.14) | non-fusion elementwise | flops 128 | bytes 1024 | tf_op jit(solution)/shard_map/convert_element_type | solution.py:67
  1.3 0.7 %fusion.3 = (f32[1536]{0:T(1024)S(1)}, f32[1536]{0:T(1024)S(1)}) fusion(bf16[1,1,1536]{2,1,0:T(2,128)(2,1)} %param.12), kind=kLoop, calls=%fused_computation.76 | loop fusion | flops 3072 | bytes 15360 | tf_op jit(solution)/shard_map/mul | solution.py:21
  2.1 0.1 reduce_sum.39
  2.5 1.2 %copy.14 = bf16[1,128,1536]{1,2,0:T(8,128)(2,1)S(1)} copy(bf16[1,128,1536]{2,1,0:T(8,128)(2,1)} %param.11) | data formatting | bytes 786432 | tf_op args[0]
  3.8 0.1 fusion.2
  4.0 0.4 rev.3
  4.4 0.2 copy.15
  4.6 0.8 %pad_maximum_fusion.8 = bf16[8,16,1664]{2,1,0:T(8,128)(2,1)} fusion(bf16[8,16,128]{2,1,0:T(8,128)(2,1)S(1)} %broadcast_in_dim.70, bf16[8,16,1536]{2,1,0:T(8,128)(2,1)S(1)} %bitcast.166), kind=kLoop, calls=%fused_computation.69 | loop fusion | flops 851968 | bytes 851968 | tf_op jit(solution)/shard_map/concatenate | solution.py:75
  5.4 5.2 %all-to-all-start = ((bf16[8,16,1664]{2,1,0:T(8,128)(2,1)}), bf16[8,16,1664]{2,1,0:T(8,128)(2,1)S(1)}, u32[]{:S(2)}, u32[]{:S(2)}) async-start(bf16[8,16,1664]{2,1,0:T(8,128)(2,1)} %pad_maximum_fusion.8), calls=%async_computation | async-start | bytes 851968 | tf_op jit(solution)/shard_map/all_to_all | solution.py:78
  10.8 0.6 %fusion.4 = s32[]{:T(128)} fusion(s32[4]{0:T(128)S(1)} %convert_reduce_fusion.1), kind=kLoop, calls=%fused_computation.88 | loop fusion | flops 11 | bytes 20 | tf_op jit(solution)/shard_map/reduce_sum | solution.py:133
  12.6 0.7 %compare_reduce_fusion = (pred[]{:T(512)}, s32[]{:T(128)}) fusion(s32[4]{0:T(128)S(1)} %convert_reduce_fusion.1), kind=kLoop, calls=%fused_computation.84 | loop fusion | flops 25 | bytes 21 | tf_op jit(solution)/shard_map/body/reduce | solution.py:137
  13.9 5.3 %all-to-all-done = bf16[8,16,1664]{2,1,0:T(8,128)(2,1)S(1)} async-done(((bf16[8,16,1664]{2,1,0:T(8,128)(2,1)}), bf16[8,16,1664]{2,1,0:T(8,128)(2,1)S(1)}, u32[]{:S(2)}, u32[]{:S(2)}) %all-to-all-start) | async-done | bytes 426016 | tf_op jit(solution)/shard_map/all_to_all | solution.py:78
  19.3 22.6 %conditional.1 = (bf16[4,4,16,1536]{3,2,0,1:T(8,128)(2,1)S(1)}) conditional(s32[]{:T(128)} %clamp.43, (s32[]{:T(128)}, pred[4,2]{0,1:T(4,128)(4,1)S(1)}, bf16[4,2,16,1536]{3,2,1,0:T(8,128)(2,1)S(1)}, s32[4]{0:T(128)S(1)}) %tuple.31, (s32[4]{0:T(128)S(1)}, s32[]{:T(128)}, bf16[4,2,16,1536]{3,2,1,0:T(8,128)(2,1)S(1)}, ...), branch_computations={%region_6.8_spmd, %region_8.10_spmd, %region_10.12_spmd, %region_1... | conditional | flops 3539008 | bytes 11600785 | solution.py:140
  19.3 0.1 copy.16
  19.4 0.7 %bitcast_reduce_fusion = (pred[]{:T(512)}, s32[]{:T(128)}) fusion(pred[4,2]{1,0:T(4,128)(4,1)S(1)} %copy.16, s32[]{:T(128)S(6)} %select_n.158), kind=kLoop, calls=%fused_computation.8 | loop fusion | flops 7 | bytes 11 | tf_op jit(solution)/shard_map/cond/branch_0_fun/reduce | solution.py:115
  22.0 3.7 %collective-permute-start.2 = (bf16[4,16,1536]{2,1,0:T(8,128)(2,1)S(1)}, bf16[4,16,1536]{2,1,0:T(8,128)(2,1)S(1)}, u32[]{:S(2)}, u32[]{:S(2)}) collective-permute-start(bf16[4,16,1536]{2,1,0:T(8,128)(2,1)S(1)} %get-tuple-element.134), channel_id=1, source_target_pairs={{0,6},{2,0},{4,2},{6,4},{1,7},{3,1},{5,3},{7,5},{8,14},{10,8},{12,... | collective-permute-start | bytes 589832 | tf_op jit(solution)/shard_map/cond/branch_0_fun/ppermute | solution.py:97
  25.7 1.0 %collective-permute-start = (bf16[4,16,1536]{2,1,0:T(8,128)(2,1)S(1)}, bf16[4,16,1536]{2,1,0:T(8,128)(2,1)S(1)}, u32[]{:S(2)}, u32[]{:S(2)}) collective-permute-start(bf16[4,16,1536]{2,1,0:T(8,128)(2,1)S(1)} %get-tuple-element.134), channel_id=1, source_target_pairs={{0,2},{2,4},{4,6},{6,0},{1,3},{3,5},{5,7},{7,1},{8,10},{10,12},{12... | collective-permute-start | bytes 589832 | tf_op jit(solution)/shard_map/cond/branch_0_fun/ppermute | solution.py:97
  26.7 0.7 %fusion.5 = (s32[1]{0:T(128)}, s32[1]{0:T(128)}, s32[1]{0:T(128)}, s32[1]{0:T(128)}) fusion(s32[4]{0:T(128)S(1)} %get-tuple-element.72), kind=kLoop, calls=%fused_computation.90 | loop fusion | bytes 32 | tf_op jit(solution)/shard_map/cond/branch_0_fun/slice | solution.py:104
  29.9 1.1 %collective-permute-done.2 = bf16[4,16,1536]{2,1,0:T(8,128)(2,1)S(1)} collective-permute-done((bf16[4,16,1536]{2,1,0:T(8,128)(2,1)S(1)}, bf16[4,16,1536]{2,1,0:T(8,128)(2,1)S(1)}, u32[]{:S(2)}, u32[]{:S(2)}) %collective-permute-start.2) | collective-permute-done | bytes 196640 | tf_op jit(solution)/shard_map/cond/branch_0_fun/ppermute | solution.py:97
  31.0 10.4 %collective-permute-done.1 = bf16[4,16,1536]{2,1,0:T(8,128)(2,1)S(1)} collective-permute-done((bf16[4,16,1536]{2,1,0:T(8,128)(2,1)S(1)}, bf16[4,16,1536]{2,1,0:T(8,128)(2,1)S(1)}, u32[]{:S(2)}, u32[]{:S(2)}) %collective-permute-start.1) | collective-permute-done | bytes 196640 | tf_op jit(solution)/shard_map/cond/branch_0_fun/ppermute | solution.py:97
  42.2 2.0 %collective-permute-done.30 = bf16[4,4,16,1536]{3,2,0,1:T(8,128)(2,1)S(1)} collective-permute-done((bf16[4,4,16,1536]{3,2,0,1:T(8,128)(2,1)S(1)}, bf16[4,4,16,1536]{3,2,0,1:T(8,128)(2,1)S(1)}, u32[]{:S(2)}, u32[]{:S(2)}) %collective-permute-start.30) | collective-permute-done | bytes 786464 | tf_op jit(solution)/shard_map/ppermute | solution.py:143
  44.2 0.7 %maximum_select_fusion.4 = bf16[4,4,32,1536]{3,2,0,1:T(8,128)(2,1)S(1)} fusion(bf16[4,4,16,1536]{3,2,0,1:T(8,128)(2,1)S(1)} %collective-permute-done.30, bf16[4,4,16,1536]{3,2,0,1:T(8,128)(2,1)S(1)} %get-tuple-element.201, pred[]{:T(512)S(6)} %eq.82), kind=kLoop, calls=%fused_computation.63 | loop fusion | flops 7077888 | bytes 3145729 | tf_op jit(solution)/shard_map/jit(_where)/select_n | solution.py:144
  44.9 0.1 copy.21
  45.0 4.7 %shard_map.55 = f32[128,1,1501]{2,1,0:T(1,128)} custom-call(bf16[4,128,1536]{2,1,0:T(8,128)(2,1)S(1)} %bitcast.161, f32[4,1,3072]{2,1,0:T(1,128)S(1)} %reshape.186.p_ref), custom_call_target="tpu_custom_call" | custom-call | tf_op jit(solution)/shard_map/pallas_call | solution.py:47
  (31 shorter events, 1.3 us)
Async XLA Ops:
  4.0 6.6 %copy-start = (s32[4]{0:T(128)S(1)}, s32[4]{0:T(128)}, u32[]{:S(2)}) copy-start(s32[4]{0:T(128)} %param.13) | copy-start | bytes 52
  5.4 13.9 %all-to-all-start = ((bf16[8,16,1664]{2,1,0:T(8,128)(2,1)}), bf16[8,16,1664]{2,1,0:T(8,128)(2,1)S(1)}, u32[]{:S(2)}, u32[]{:S(2)}) async-start(bf16[8,16,1664]{2,1,0:T(8,128)(2,1)} %pad_maximum_fusion.8), calls=%async_computation | async-start | bytes 851968 | tf_op jit(solution)/shard_map/all_to_all | solution.py:78
  22.0 9.0 %collective-permute-start.2 = (bf16[4,16,1536]{2,1,0:T(8,128)(2,1)S(1)}, bf16[4,16,1536]{2,1,0:T(8,128)(2,1)S(1)}, u32[]{:S(2)}, u32[]{:S(2)}) collective-permute-start(bf16[4,16,1536]{2,1,0:T(8,128)(2,1)S(1)} %get-tuple-element.134), channel_id=1, source_target_pairs={{0,6},{2,0},{4,2},{6,4},{1,7},{3,1},{5,3},{7,5},{8,14},{10,8},{12,... | collective-permute-start | bytes 589832 | tf_op jit(solution)/shard_map/cond/branch_0_fun/ppermute | solution.py:97
  25.7 15.7 %collective-permute-start.1 = (bf16[4,16,1536]{2,1,0:T(8,128)(2,1)S(1)}, bf16[4,16,1536]{2,1,0:T(8,128)(2,1)S(1)}, u32[]{:S(2)}, u32[]{:S(2)}) collective-permute-start(bf16[4,16,1536]{2,1,0:T(8,128)(2,1)S(1)} %get-tuple-element.134), channel_id=1, source_target_pairs={{0,4},{2,6},{4,0},{6,2},{1,5},{3,7},{5,1},{7,3},{8,12},{10,14},{12... | collective-permute-start | bytes 589832 | tf_op jit(solution)/shard_map/cond/branch_0_fun/ppermute | solution.py:97
  25.7 15.7 %collective-permute-start = (bf16[4,16,1536]{2,1,0:T(8,128)(2,1)S(1)}, bf16[4,16,1536]{2,1,0:T(8,128)(2,1)S(1)}, u32[]{:S(2)}, u32[]{:S(2)}) collective-permute-start(bf16[4,16,1536]{2,1,0:T(8,128)(2,1)S(1)} %get-tuple-element.134), channel_id=1, source_target_pairs={{0,2},{2,4},{4,6},{6,0},{1,3},{3,5},{5,7},{7,1},{8,10},{10,12},{12... | collective-permute-start | bytes 589832 | tf_op jit(solution)/shard_map/cond/branch_0_fun/ppermute | solution.py:97
  41.9 2.4 %collective-permute-start.30 = (bf16[4,4,16,1536]{3,2,0,1:T(8,128)(2,1)S(1)}, bf16[4,4,16,1536]{3,2,0,1:T(8,128)(2,1)S(1)}, u32[]{:S(2)}, u32[]{:S(2)}) collective-permute-start(bf16[4,4,16,1536]{3,2,0,1:T(8,128)(2,1)S(1)} %get-tuple-element.201), channel_id=1, source_target_pairs={{0,1},{1,0},{2,3},{3,2},{4,5},{5,4},{6,7},{7,6},{8,9},{9,8},{10,11... | collective-permute-start | bytes 2359304 | tf_op jit(solution)/shard_map/ppermute | solution.py:143
where the time goes:
time: 50.2 us; the launch traced here: 49.8 us
  waiting for transfers between devices  18.8 us (37%)
  starting transfers between devices  9.94 us (20%)
  other arithmetic  5.68 us (11%)
  Pallas kernels  4.75 us (9%)
  loops' own time  4.73 us (9%)
  local copies, waits for them, and re-layouts  3.25 us (6%)
  between operations  2.6 us (5%)
    ppermute x3, waiting for transfers between devices, ring_of(): lax.ppermute(part, 'zz', [(i, (i + j) % n_chip) for i in range(n_chip)])  11.5 us
    all_to_all x1, waiting for transfers between devices, body(): got = lax.all_to_all(payload, ('win', 'core'), 0, 0, tiled=True)  5.35 us
    all_to_all x1, starting transfers between devices, body(): got = lax.all_to_all(payload, ('win', 'core'), 0, 0, tiled=True)  5.2 us
    pallas_call x1, Pallas kernels, correlate(): pl.pallas_call(kern, out_shape=jax.ShapeDtypeStruct((m, 1, lags), jnp.flo...  4.75 us
    another operation x1, loops' own time, body(): mine_half = lax.switch(which, branches, src)  4.73 us
    ppermute x3, starting transfers between devices, ring_of(): lax.ppermute(part, 'zz', [(i, (i + j) % n_chip) for i in range(n_chip)])  4.67 us
    ppermute x1, waiting for transfers between devices, body(): other_half = lax.ppermute(mine_half, 'core', [(0, 1), (1, 0)])  2.01 us
    unnamed x3, local copies, waits for them, and re-layouts  1.23 us
  transfers between devices with their start and end apart: 5, of which 4 were waited for; matrix products, arithmetic and copies ran while one was open for 5% of the time, Pallas kernels for 0%

commit v1 on v0

--- a/solution.py
+++ b/solution.py
@@ -33,7 +33,7 @@
             v = p_ref[w, :, start:start + width]
             rows = jnp.broadcast_to(v, (CHUNK, width))
             rolled = pltpu.roll(rows, 0, 1, stride=1, stride_axis=0)
-            band = rolled[:, CHUNK:CHUNK + cols].astype(jnp.bfloat16)
+            band = rolled[:, CHUNK:CHUNK + cols]
             acc = acc + jnp.dot(
                 x_ref[w, :, t0:t0 + CHUNK], band, preferred_element_type=jnp.float32
             )
@@ -151,7 +151,7 @@
     mine = lax.dynamic_index_in_dim(got, my_core, axis=1, keepdims=False)
     rcv_all = mine[:, :, nt:nt + per].reshape(n_win, half * per)[:, :nt]
     padded = jnp.pad(
-        rcv_all.astype(jnp.float32), ((0, 0), (HALF + 1, cols - HALF - 1))
+        rcv_all, ((0, 0), (HALF + 1, cols - HALF - 1))
     )[:, None, :]
 
     out = correlate(x, padded, lag_count, scale)

time: 50.2 us -> 49.4 us (0.984)
  Pallas kernels: 4.75 us -> 4.17 us
    pallas_call x1, Pallas kernels: 4.75 us -> 4.17 us  [correlate(): pl.pallas_call(kern, out_shape=jax.ShapeDtypeStruct((m, 1, lags), jnp.flo...]
where the time goes in v1:
time: 49.4 us; the launch traced here: 49 us
  waiting for transfers between devices  18.8 us (38%)
  starting transfers between devices  9.94 us (20%)
  other arithmetic  5.6 us (11%)
  loops' own time  4.55 us (9%)
  Pallas kernels  4.17 us (8%)
  local copies, waits for them, and re-layouts  3.34 us (7%)
  between operations  2.6 us (5%)
    ppermute x3, waiting for transfers between devices, ring_of(): lax.ppermute(part, 'zz', [(i, (i + j) % n_chip) for i in range(n_chip)])  11.5 us
    all_to_all x1, waiting for transfers between devices, body(): got = lax.all_to_all(payload, ('win', 'core'), 0, 0, tiled=True)  5.35 us
    all_to_all x1, starting transfers between devices, body(): got = lax.all_to_all(payload, ('win', 'core'), 0, 0, tiled=True)  5.2 us
    ppermute x3, starting transfers between devices, ring_of(): lax.ppermute(part, 'zz', [(i, (i + j) % n_chip) for i in range(n_chip)])  4.67 us
    another operation x1, loops' own time, body(): mine_half = lax.switch(which, branches, src)  4.55 us
    pallas_call x1, Pallas kernels, correlate(): pl.pallas_call(kern, out_shape=jax.ShapeDtypeStruct((m, 1, lags), jnp.flo...  4.17 us
    ppermute x1, waiting for transfers between devices, body(): other_half = lax.ppermute(mine_half, 'core', [(0, 1), (1, 0)])  2 us
    unnamed x3, local copies, waits for them, and re-layouts  1.23 us
  transfers between devices with their start and end apart: 5, of which 4 were waited for; matrix products, arithmetic and copies ran while one was open for 5% of the time, Pallas kernels for 0%

profile of v1, /device:TPU:0, one launch (start us, length us, event | category | flops | bytes accessed | tf_op | source)
XLA Modules:
  0.0 49.0 jit_solution(17506476330432348380)
XLA Ops:
  0.7 0.7 %convert_element_type.73 = f32[128]{0:T(128)S(1)} convert(s32[128]{0:T(128)} %param.14) | non-fusion elementwise | flops 128 | bytes 1024 | tf_op jit(solution)/shard_map/convert_element_type | solution.py:67
  1.3 0.7 %fusion.3 = (f32[1536]{0:T(1024)S(1)}, f32[1536]{0:T(1024)S(1)}) fusion(bf16[1,1,1536]{2,1,0:T(2,128)(2,1)} %param.12), kind=kLoop, calls=%fused_computation.76 | loop fusion | flops 3072 | bytes 15360 | tf_op jit(solution)/shard_map/mul | solution.py:21
  2.1 0.1 reduce_sum.39
  2.5 1.2 %copy.16 = bf16[1,128,1536]{1,2,0:T(8,128)(2,1)S(1)} copy(bf16[1,128,1536]{2,1,0:T(8,128)(2,1)} %param.11) | data formatting | bytes 786432 | tf_op args[0]
  3.8 0.1 fusion.2
  4.0 0.4 rev.3
  4.4 0.2 copy.17
  4.6 0.8 %pad_maximum_fusion.8 = bf16[8,16,1664]{2,1,0:T(8,128)(2,1)} fusion(bf16[8,16,128]{2,1,0:T(8,128)(2,1)S(1)} %broadcast_in_dim.68, bf16[8,16,1536]{2,1,0:T(8,128)(2,1)S(1)} %bitcast.168), kind=kLoop, calls=%fused_computation.69 | loop fusion | flops 851968 | bytes 851968 | tf_op jit(solution)/shard_map/concatenate | solution.py:75
  5.4 5.2 %all-to-all-start = ((bf16[8,16,1664]{2,1,0:T(8,128)(2,1)}), bf16[8,16,1664]{2,1,0:T(8,128)(2,1)S(1)}, u32[]{:S(2)}, u32[]{:S(2)}) async-start(bf16[8,16,1664]{2,1,0:T(8,128)(2,1)} %pad_maximum_fusion.8), calls=%async_computation | async-start | bytes 851968 | tf_op jit(solution)/shard_map/all_to_all | solution.py:78
  10.8 0.6 %fusion.4 = s32[]{:T(128)} fusion(s32[4]{0:T(128)S(1)} %convert_reduce_fusion.1), kind=kLoop, calls=%fused_computation.88 | loop fusion | flops 11 | bytes 20 | tf_op jit(solution)/shard_map/reduce_sum | solution.py:133
  12.6 0.7 %compare_reduce_fusion = (pred[]{:T(512)}, s32[]{:T(128)}) fusion(s32[4]{0:T(128)S(1)} %convert_reduce_fusion.1), kind=kLoop, calls=%fused_computation.84 | loop fusion | flops 25 | bytes 21 | tf_op jit(solution)/shard_map/body/reduce | solution.py:137
  13.9 5.3 %all-to-all-done = bf16[8,16,1664]{2,1,0:T(8,128)(2,1)S(1)} async-done(((bf16[8,16,1664]{2,1,0:T(8,128)(2,1)}), bf16[8,16,1664]{2,1,0:T(8,128)(2,1)S(1)}, u32[]{:S(2)}, u32[]{:S(2)}) %all-to-all-start) | async-done | bytes 426016 | tf_op jit(solution)/shard_map/all_to_all | solution.py:78
  19.3 22.4 %conditional.1 = (bf16[4,4,16,1536]{3,2,0,1:T(8,128)(2,1)S(1)}) conditional(s32[]{:T(128)} %clamp.43, (s32[]{:T(128)}, pred[4,2]{0,1:T(4,128)(4,1)S(1)}, bf16[4,2,16,1536]{3,2,1,0:T(8,128)(2,1)S(1)}, s32[4]{0:T(128)S(1)}) %tuple.31, (s32[4]{0:T(128)S(1)}, s32[]{:T(128)}, bf16[4,2,16,1536]{3,2,1,0:T(8,128)(2,1)S(1)}, ...), branch_computations={%region_6.8_spmd, %region_8.10_spmd, %region_10.12_spmd, %region_1... | conditional | flops 3539008 | bytes 11600785 | solution.py:140
  19.3 0.1 copy.18
  19.4 0.7 %bitcast_reduce_fusion = (pred[]{:T(512)}, s32[]{:T(128)}) fusion(pred[4,2]{1,0:T(4,128)(4,1)S(1)} %copy.18, s32[]{:T(128)S(6)} %select_n.158), kind=kLoop, calls=%fused_computation.8 | loop fusion | flops 7 | bytes 11 | tf_op jit(solution)/shard_map/cond/branch_0_fun/reduce | solution.py:115
  22.0 3.7 %collective-permute-start.2 = (bf16[4,16,1536]{2,1,0:T(8,128)(2,1)S(1)}, bf16[4,16,1536]{2,1,0:T(8,128)(2,1)S(1)}, u32[]{:S(2)}, u32[]{:S(2)}) collective-permute-start(bf16[4,16,1536]{2,1,0:T(8,128)(2,1)S(1)} %get-tuple-element.134), channel_id=1, source_target_pairs={{0,6},{2,0},{4,2},{6,4},{1,7},{3,1},{5,3},{7,5},{8,14},{10,8},{12,... | collective-permute-start | bytes 589832 | tf_op jit(solution)/shard_map/cond/branch_0_fun/ppermute | solution.py:97
  25.7 1.0 %collective-permute-start = (bf16[4,16,1536]{2,1,0:T(8,128)(2,1)S(1)}, bf16[4,16,1536]{2,1,0:T(8,128)(2,1)S(1)}, u32[]{:S(2)}, u32[]{:S(2)}) collective-permute-start(bf16[4,16,1536]{2,1,0:T(8,128)(2,1)S(1)} %get-tuple-element.134), channel_id=1, source_target_pairs={{0,2},{2,4},{4,6},{6,0},{1,3},{3,5},{5,7},{7,1},{8,10},{10,12},{12... | collective-permute-start | bytes 589832 | tf_op jit(solution)/shard_map/cond/branch_0_fun/ppermute | solution.py:97
  26.7 0.7 %fusion.5 = (s32[1]{0:T(128)}, s32[1]{0:T(128)}, s32[1]{0:T(128)}, s32[1]{0:T(128)}) fusion(s32[4]{0:T(128)S(1)} %get-tuple-element.72), kind=kLoop, calls=%fused_computation.90 | loop fusion | bytes 32 | tf_op jit(solution)/shard_map/cond/branch_0_fun/slice | solution.py:104
  29.9 1.1 %collective-permute-done.2 = bf16[4,16,1536]{2,1,0:T(8,128)(2,1)S(1)} collective-permute-done((bf16[4,16,1536]{2,1,0:T(8,128)(2,1)S(1)}, bf16[4,16,1536]{2,1,0:T(8,128)(2,1)S(1)}, u32[]{:S(2)}, u32[]{:S(2)}) %collective-permute-start.2) | collective-permute-done | bytes 196640 | tf_op jit(solution)/shard_map/cond/branch_0_fun/ppermute | solution.py:97
  31.0 10.4 %collective-permute-done.1 = bf16[4,16,1536]{2,1,0:T(8,128)(2,1)S(1)} collective-permute-done((bf16[4,16,1536]{2,1,0:T(8,128)(2,1)S(1)}, bf16[4,16,1536]{2,1,0:T(8,128)(2,1)S(1)}, u32[]{:S(2)}, u32[]{:S(2)}) %collective-permute-start.1) | collective-permute-done | bytes 196640 | tf_op jit(solution)/shard_map/cond/branch_0_fun/ppermute | solution.py:97
  42.1 2.0 %collective-permute-done.30 = bf16[4,4,16,1536]{3,2,0,1:T(8,128)(2,1)S(1)} collective-permute-done((bf16[4,4,16,1536]{3,2,0,1:T(8,128)(2,1)S(1)}, bf16[4,4,16,1536]{3,2,0,1:T(8,128)(2,1)S(1)}, u32[]{:S(2)}, u32[]{:S(2)}) %collective-permute-start.30) | collective-permute-done | bytes 786464 | tf_op jit(solution)/shard_map/ppermute | solution.py:143
  44.1 0.7 %maximum_select_fusion.4 = bf16[4,4,32,1536]{3,2,0,1:T(8,128)(2,1)S(1)} fusion(bf16[4,4,16,1536]{3,2,0,1:T(8,128)(2,1)S(1)} %collective-permute-done.30, bf16[4,4,16,1536]{3,2,0,1:T(8,128)(2,1)S(1)} %get-tuple-element.201, pred[]{:T(512)S(6)} %eq.82), kind=kLoop, calls=%fused_computation.63 | loop fusion | flops 7077888 | bytes 3145729 | tf_op jit(solution)/shard_map/jit(_where)/select_n | solution.py:144
  44.7 0.1 copy.23
  44.8 4.2 %shard_map.55 = f32[128,1,1501]{2,1,0:T(1,128)} custom-call(bf16[4,128,1536]{2,1,0:T(8,128)(2,1)S(1)} %bitcast.163, bf16[4,1,3072]{2,1,0:T(2,128)(2,1)S(1)} %copy.24.p_ref), custom_call_target="tpu_custom_call" | custom-call | tf_op jit(solution)/shard_map/pallas_call | solution.py:47
  (31 shorter events, 1.3 us)
Async XLA Ops:
  4.0 6.6 %copy-start = (s32[4]{0:T(128)S(1)}, s32[4]{0:T(128)}, u32[]{:S(2)}) copy-start(s32[4]{0:T(128)} %param.13) | copy-start | bytes 52
  5.4 13.9 %all-to-all-start = ((bf16[8,16,1664]{2,1,0:T(8,128)(2,1)}), bf16[8,16,1664]{2,1,0:T(8,128)(2,1)S(1)}, u32[]{:S(2)}, u32[]{:S(2)}) async-start(bf16[8,16,1664]{2,1,0:T(8,128)(2,1)} %pad_maximum_fusion.8), calls=%async_computation | async-start | bytes 851968 | tf_op jit(solution)/shard_map/all_to_all | solution.py:78
  22.0 9.0 %collective-permute-start.2 = (bf16[4,16,1536]{2,1,0:T(8,128)(2,1)S(1)}, bf16[4,16,1536]{2,1,0:T(8,128)(2,1)S(1)}, u32[]{:S(2)}, u32[]{:S(2)}) collective-permute-start(bf16[4,16,1536]{2,1,0:T(8,128)(2,1)S(1)} %get-tuple-element.134), channel_id=1, source_target_pairs={{0,6},{2,0},{4,2},{6,4},{1,7},{3,1},{5,3},{7,5},{8,14},{10,8},{12,... | collective-permute-start | bytes 589832 | tf_op jit(solution)/shard_map/cond/branch_0_fun/ppermute | solution.py:97
  25.7 15.7 %collective-permute-start.1 = (bf16[4,16,1536]{2,1,0:T(8,128)(2,1)S(1)}, bf16[4,16,1536]{2,1,0:T(8,128)(2,1)S(1)}, u32[]{:S(2)}, u32[]{:S(2)}) collective-permute-start(bf16[4,16,1536]{2,1,0:T(8,128)(2,1)S(1)} %get-tuple-element.134), channel_id=1, source_target_pairs={{0,4},{2,6},{4,0},{6,2},{1,5},{3,7},{5,1},{7,3},{8,12},{10,14},{12... | collective-permute-start | bytes 589832 | tf_op jit(solution)/shard_map/cond/branch_0_fun/ppermute | solution.py:97
  25.7 15.7 %collective-permute-start = (bf16[4,16,1536]{2,1,0:T(8,128)(2,1)S(1)}, bf16[4,16,1536]{2,1,0:T(8,128)(2,1)S(1)}, u32[]{:S(2)}, u32[]{:S(2)}) collective-permute-start(bf16[4,16,1536]{2,1,0:T(8,128)(2,1)S(1)} %get-tuple-element.134), channel_id=1, source_target_pairs={{0,2},{2,4},{4,6},{6,0},{1,3},{3,5},{5,7},{7,1},{8,10},{10,12},{12... | collective-permute-start | bytes 589832 | tf_op jit(solution)/shard_map/cond/branch_0_fun/ppermute | solution.py:97
  41.7 2.4 %collective-permute-start.30 = (bf16[4,4,16,1536]{3,2,0,1:T(8,128)(2,1)S(1)}, bf16[4,4,16,1536]{3,2,0,1:T(8,128)(2,1)S(1)}, u32[]{:S(2)}, u32[]{:S(2)}) collective-permute-start(bf16[4,4,16,1536]{3,2,0,1:T(8,128)(2,1)S(1)} %get-tuple-element.201), channel_id=1, source_target_pairs={{0,1},{1,0},{2,3},{3,2},{4,5},{5,4},{6,7},{7,6},{8,9},{9,8},{10,11... | collective-permute-start | bytes 2359304 | tf_op jit(solution)/shard_map/ppermute | solution.py:143
